TPU v7x, 512 devices: a whole 4x4x16 slice. The times are simulated.
512 devices in a mesh: gx: 16 (over z), gy: 8 (over y, x_lo), gz: 4 (over x_hi, core).
Axes of the slice: x: 4 (x_hi: 2, x_lo: 2; x = x_hi * 2 + x_lo), y: 4, z: 16, core: 2. Of those that a mesh axis runs over, the one named last changes fastest.
Arguments:
- velocity: float32 [3, 128, 64, 512], P(None, 'gx', 'gy', 'gz'), may hold values from -4 to 4
- sketch_prev: float32 [3, 64, 4, 32, 32, 128], P(None, 'gy', 'gz', 'gx'), may hold values from -6 to 6
- seed_matrix: int32 [512, 128], replicated, may hold values from -4 to 4
- snap_steps: int32 [4], replicated, may hold values from 0 to 511
- rank_keep: int32 [1], replicated, may hold values from 32 to 128
Outputs:
- velocity_out: float32 [3, 128, 64, 512], P(None, 'gx', 'gy', 'gz')
- mode_rows: float32 [3, 64, 4, 32, 32, 128], P(None, 'gy', 'gz', 'gx')
- factor: float32 [128, 128], replicated
All inputs are finite; a program needn't handle non-finite values.
Results may differ from a plain program's by a relative error of at most 0.0003.
Values sent between devices are 32-bit elements; how exact they have to be, the bound alone decides.
No kernel may reach another device: no remote copies, remote signals or barrier semaphores. Data moves between devices by JAX's collectives and lax.ppermute only.
A program may use at most 64 MiB of HBM per device.

v0:
```python
import math
import jax
import jax.numpy as jnp
from jax import lax
from jax.sharding import PartitionSpec as P

SNAPS = 4
STEPS = 2
TIME_STEP = 0.1
VISCOSITY = 0.4
ONE_THIRD = 1.0 / 3.0
TWO_THIRDS = 2.0 / 3.0
HIGHEST = lax.Precision.HIGHEST


def extended(block, sides, width):
    for axis, dim in sides:
        count = lax.axis_size(axis)
        forward = [(i, i + 1) for i in range(count - 1)]
        forward.append((count - 1, 0))
        backward = [(target, source) for source, target in forward]
        low = lax.ppermute(
            lax.slice_in_dim(block, block.shape[dim] - width, None, axis=dim), axis, forward
        )
        high = lax.ppermute(lax.slice_in_dim(block, 0, width, axis=dim), axis, backward)
        block = jnp.concatenate([low, block, high], axis=dim)
    return block


def tendency(padded):
    center = padded[:, 1:-1, 1:-1, 1:-1]
    forward = (padded[:, 2:, 1:-1, 1:-1], padded[:, 1:-1, 2:, 1:-1], padded[:, 1:-1, 1:-1, 2:])
    backward = (padded[:, :-2, 1:-1, 1:-1], padded[:, 1:-1, :-2, 1:-1], padded[:, 1:-1, 1:-1, :-2])
    convect = (
        center[0:1] * (forward[0] - backward[0])
        + center[1:2] * (forward[1] - backward[1])
        + center[2:3] * (forward[2] - backward[2])
    )
    spread = (
        forward[0]
        + backward[0]
        + forward[1]
        + backward[1]
        + forward[2]
        + backward[2]
        - 6.0 * center
    )
    return -0.5 * convect + VISCOSITY * spread


def with_walls(padded, margin):
    cells_y = padded.shape[2] - 2 * margin
    wall_rows = (
        lax.axis_index("gy") * cells_y - margin + jnp.arange(cells_y + 2 * margin, dtype=jnp.int32)
    )
    inside = ((wall_rows >= 0) & (wall_rows < lax.axis_size("gy") * cells_y)).astype(jnp.float32)
    return padded * inside[None, None, :, None]


def faces_padded(current):
    return with_walls(extended(current, (("gx", 1), ("gy", 2), ("gz", 3)), 1), 1)


def step_by_section(current):
    first_section = current + TIME_STEP * tendency(faces_padded(current))
    second_section = 0.75 * current + 0.25 * (
        first_section + TIME_STEP * tendency(faces_padded(first_section))
    )
    return ONE_THIRD * current + TWO_THIRDS * (
        second_section + TIME_STEP * tendency(faces_padded(second_section))
    )


def coarse_local(current):
    cells_x = current.shape[1]
    cells_y = current.shape[2]
    cells_z = current.shape[3]
    blocks = current.reshape(3, cells_x // 4, 4, cells_y, cells_z // 4, 4)
    return jnp.transpose(jnp.mean(blocks, axis=(2, 5)), (0, 2, 3, 1))


def on_device(velocity, sketch_prev, seed_matrix, snap_steps, rank_keep):
    current = velocity
    collected = []
    for snap_index in range(SNAPS):
        for step_index in range(STEPS):
            current = step_by_section(current)
        local_snap = coarse_local(current)
        collected.append(lax.all_to_all(local_snap, "gx", split_axis=2, concat_axis=3, tiled=True))
    stacked = jnp.stack(collected)
    rank_total = sketch_prev.shape[-1]
    snap_rows = stacked.reshape(stacked.shape[0], -1)
    picker = (
        snap_steps[:, None] == jnp.arange(seed_matrix.shape[0], dtype=jnp.int32)[None, :]
    ).astype(jnp.float32)
    omega_rows = 0.5 * jnp.dot(picker, seed_matrix.astype(jnp.float32), precision=HIGHEST)
    sketch_rows = sketch_prev.reshape(-1, rank_total) + lax.dot_general(
        snap_rows, omega_rows, (((0,), (0,)), ((), ())), precision=HIGHEST
    )
    local_gram = lax.dot_general(
        sketch_rows, sketch_rows, (((0,), (0,)), ((), ())), precision=HIGHEST
    )
    gram_sum = lax.psum(local_gram, ("gx", "gy", "gz"))
    lower_factor = jnp.linalg.cholesky(gram_sum)
    identity = jnp.eye(rank_total, dtype=jnp.float32)
    inverse = lax.linalg.triangular_solve(lower_factor, identity, left_side=True, lower=True).T
    total_rows = (
        sketch_rows.shape[0] * lax.axis_size("gx") * lax.axis_size("gy") * lax.axis_size("gz")
    )
    norm_scale = math.sqrt(total_rows)
    inside = (jnp.arange(rank_total, dtype=jnp.int32) < rank_keep[0]).astype(jnp.float32)
    mode_rows = norm_scale * jnp.dot(sketch_rows, inverse, precision=HIGHEST) * inside[None, :]
    factor = lower_factor.T * (1.0 / norm_scale) * inside[:, None] * inside[None, :]
    return (current, mode_rows.reshape(sketch_prev.shape), factor)


def solution(mesh):
    placed = (P(None, "gx", "gy", "gz"), P(None, "gy", "gz", "gx", None, None), P(), P(), P())
    return jax.shard_map(
        on_device,
        mesh=mesh,
        in_specs=placed,
        out_specs=(P(None, "gx", "gy", "gz"), P(None, "gy", "gz", "gx", None, None), P()),
        check_vma=False,
    )
```

profile of v0, /device:TPU:1, one launch (start us, length us, event | category | flops | bytes accessed | tf_op | source)
XLA Modules:
  0.0 1293.1 jit_solution(17506120628596611169)
XLA Ops:
  12.3 9.5 collective-permute-start.1
  31.3 7.0 collective-permute-start.4
  41.4 5.9 collective-permute-done.5
  50.0 5.1 collective-permute-start.7
  71.5 5.9 collective-permute-done.11
  80.1 5.1 collective-permute-start.13
  88.3 5.2 collective-permute-start.15
  101.7 5.9 collective-permute-done.17
  110.4 5.0 collective-permute-start.19
  119.0 4.6 collective-permute-start.21
  131.8 5.9 collective-permute-done.23
  148.8 5.4 collective-permute-start.27
  162.7 5.9 collective-permute-done.29
  169.4 4.9 collective-permute-start.30
  181.3 5.1 collective-permute-start.33
  194.8 5.9 collective-permute-done.35
  211.8 5.5 collective-permute-start.39
  225.8 5.9 collective-permute-done.41
  242.5 5.5 collective-permute-start.45
  249.0 4.6 collective-permute-start.46
  256.7 5.9 collective-permute-done.47
  272.6 5.5 collective-permute-start.51
  279.1 4.6 collective-permute-start.52
  286.8 5.9 collective-permute-done.53
  303.0 5.5 collective-permute-start.57
  316.9 5.9 collective-permute-done.59
  333.2 5.4 collective-permute-start.63
  347.0 5.9 collective-permute-done.65
  363.3 5.5 collective-permute-start.69
  369.8 4.6 collective-permute-start.70
  377.5 5.9 collective-permute-done.71
  393.5 5.5 collective-permute-start.75
  400.0 4.6 collective-permute-start.76
  407.7 5.9 collective-permute-done.77
  423.9 5.5 collective-permute-start.81
  437.8 5.9 collective-permute-done.83
  454.1 5.4 collective-permute-start.87
  467.9 5.9 collective-permute-done.89
  484.1 5.5 collective-permute-start.93
  498.0 5.9 collective-permute-done.95
  514.2 5.5 collective-permute-start.99
  528.2 5.9 collective-permute-done.101
  544.4 5.5 collective-permute-start.105
  558.3 5.9 collective-permute-done.107
  574.5 5.5 collective-permute-start.111
  588.4 5.9 collective-permute-done.113
  604.9 5.7 collective-permute-start.117
  618.9 5.9 collective-permute-done.119
  635.8 5.5 collective-permute-start.123
  649.8 5.9 collective-permute-done.125
  666.8 5.5 collective-permute-start.129
  680.7 5.9 collective-permute-done.131
  697.7 5.5 collective-permute-start.135
  711.6 5.9 collective-permute-done.137
  725.5 6.0 all-to-all-start
  734.5 5.5 collective-permute-start.141
  748.1 5.9 collective-permute-done.143
  754.5 11.8 all-to-all-start.1
  767.5 11.1 all-to-all-done.1
  782.8 11.6 all-to-all-done.2
  801.6 8.7 all-to-all-done.3
  814.8 443.6 %all-reduce.2.cloned.1.call-done = f32[128,128]{0,1:T(8,128)} async-done(((f32[128,128]{0,1:T(8,128)}), f32[128,128]{0,1:T(8,128)}) %all-reduce.2.cloned.1.call-update) | async-done | bytes 65552 | tf_op jit(solution)/shard_map/psum | solution.py:103
  1260.2 11.7 cholesky.17
  1274.1 9.8 custom-call.6
  (461 shorter events, 445.5 us)
Async XLA Ops:
  8.0 13.9 %collective-permute-start = (f32[3,1,8,128]{3,2,1,0:T(8,128)S(1)}, f32[3,1,8,128]{3,2,1,0:T(8,128)S(1)}, u32[]{:S(2)}, u32[]{:S(2)}) collective-permute-start(f32[3,1,8,128]{3,2,1,0:T(8,128)S(1)} %get-tuple-element.230), channel_id=1, source_target_pairs={{0,32},{32,64},{64,96},{96,128},{128,160},{160,192},{192,224},{224... | collective-permute-start | bytes 36872 | tf_op jit(solution)/shard_map/ppermute | solution.py:22
  12.3 10.4 collective-permute-start.1
  22.8 7.5 collective-permute-start.2
  31.3 10.1 collective-permute-start.4
  38.3 9.0 collective-permute-start.5
  56.0 7.4 collective-permute-start.8
  68.4 9.0 collective-permute-start.11
  86.1 7.4 collective-permute-start.14
  98.5 9.0 collective-permute-start.17
  116.2 7.4 collective-permute-start.20
  128.7 9.0 collective-permute-start.23
  146.9 7.4 collective-permute-start.26
  155.3 7.4 collective-permute-start.28
  159.6 9.0 collective-permute-start.29
  187.4 7.4 collective-permute-start.34
  191.7 9.0 collective-permute-start.35
  218.3 7.4 collective-permute-start.40
  222.6 9.0 collective-permute-start.41
  249.0 7.7 collective-permute-start.46
  253.6 9.0 collective-permute-start.47
  270.7 7.4 collective-permute-start.50
  279.1 7.7 collective-permute-start.52
  283.7 9.0 collective-permute-start.53
  301.1 7.4 collective-permute-start.56
  309.5 7.4 collective-permute-start.58
  313.8 9.0 collective-permute-start.59
  331.2 7.4 collective-permute-start.62
  339.6 7.4 collective-permute-start.64
  343.9 9.0 collective-permute-start.65
  369.8 7.7 collective-permute-start.70
  374.4 9.0 collective-permute-start.71
  391.5 7.4 collective-permute-start.74
  400.0 7.7 collective-permute-start.76
  404.6 9.0 collective-permute-start.77
  430.4 7.4 collective-permute-start.82
  434.7 9.0 collective-permute-start.83
  460.5 7.4 collective-permute-start.88
  464.8 9.0 collective-permute-start.89
  490.6 7.4 collective-permute-start.94
  494.9 9.0 collective-permute-start.95
  520.7 7.4 collective-permute-start.100
  525.0 9.0 collective-permute-start.101
  550.9 7.4 collective-permute-start.106
  555.2 9.0 collective-permute-start.107
  581.0 7.4 collective-permute-start.112
  585.3 9.0 collective-permute-start.113
  603.0 7.6 collective-permute-start.116
  611.4 7.4 collective-permute-start.118
  615.8 9.0 collective-permute-start.119
  642.3 7.4 collective-permute-start.124
  646.7 9.0 collective-permute-start.125
  673.3 7.4 collective-permute-start.130
  677.6 9.0 collective-permute-start.131
  695.8 8.3 collective-permute-start.134
  708.5 9.0 collective-permute-start.137
  718.3 14.2 %collective-permute-start.138 = (f32[3,1,8,128]{3,2,1,0:T(8,128)S(1)}, f32[3,1,8,128]{3,2,1,0:T(8,128)S(1)}, u32[]{:S(2)}, u32[]{:S(2)}) collective-permute-start(f32[3,1,8,128]{3,2,1,0:T(8,128)S(1)} %get-tuple-element.183), channel_id=1, source_target_pairs={{0,32},{32,64},{64,96},{96,128},{128,160},{160,192},{192,224},{224... | collective-permute-start | bytes 36872 | tf_op jit(solution)/shard_map/ppermute | solution.py:22
  721.9 10.6 collective-permute-start.139
  725.5 29.0 %all-to-all-start = ((f32[3,8,32,2]{1,3,0,2:T(2,128)}), f32[3,8,32,2]{1,3,0,2:T(2,128)S(1)}, u32[]{:S(2)}, u32[]{:S(2)}) async-start(f32[3,8,32,2]{1,3,0,2:T(2,128)} %copy.41), calls=%async_computation | async-start | bytes 196608 | tf_op jit(solution)/shard_map/all_to_all | solution.py:89
  732.5 9.1 collective-permute-start.140
  745.0 9.0 collective-permute-start.143
  754.5 24.0 %all-to-all-start.1 = ((f32[3,8,32,2]{1,3,0,2:T(2,128)}), f32[3,8,32,2]{1,3,0,2:T(2,128)S(1)}, u32[]{:S(2)}, u32[]{:S(2)}) async-start(f32[3,8,32,2]{1,3,0,2:T(2,128)} %copy.45), calls=%async_computation.1 | async-start | bytes 196608 | tf_op jit(solution)/shard_map/all_to_all | solution.py:89
  778.6 15.8 %all-to-all-start.2 = ((f32[3,8,32,2]{1,3,0,2:T(2,128)}), f32[3,8,32,2]{1,3,0,2:T(2,128)S(1)}, u32[]{:S(2)}, u32[]{:S(2)}) async-start(f32[3,8,32,2]{1,3,0,2:T(2,128)} %copy.49), calls=%async_computation.2 | async-start | bytes 196608 | tf_op jit(solution)/shard_map/all_to_all | solution.py:89
  794.4 16.0 %all-to-all-start.3 = ((f32[3,8,32,2]{1,3,0,2:T(2,128)}), f32[3,8,32,2]{1,3,0,2:T(2,128)S(1)}, u32[]{:S(2)}, u32[]{:S(2)}) async-start(f32[3,8,32,2]{1,3,0,2:T(2,128)} %copy.53), calls=%async_computation.3 | async-start | bytes 196608 | tf_op jit(solution)/shard_map/all_to_all | solution.py:89
  798.5 459.9 %all-reduce.2.cloned.1.call-start = ((), (), s32[]{:S(2)}) async-start(), calls=%async_computation.4 | async-start | bytes 131072 | tf_op jit(solution)/shard_map/psum | solution.py:103
  (90 other events, 640.8 us)
Sparse Core Ops, SparseCore 0:
  814.9 443.4 all-reduce.1
where the time goes:
time: 1310 us; the launch traced here: 1290 us
  waiting for transfers between devices  687 us (52%)
  starting transfers between devices  523 us (40%)
  other arithmetic  42.5 us (3%)
  between operations  18.1 us (1%)
  local copies, waits for them, and re-layouts  17.1 us (1%)
    psum x1, waiting for transfers between devices, on_device(): gram_sum = lax.psum(local_gram, ('gx', 'gy', 'gz'))  444 us
    ppermute x72, starting transfers between devices, extended(): lax.ppermute(lax.slice_in_dim(block, 0, width, axis=dim), axis, backward)  267 us
    ppermute x72, starting transfers between devices, extended(): lax.ppermute(lax.slice_in_dim(block, block.shape[dim] - width, None, axis...  231 us
    ppermute x72, waiting for transfers between devices, extended(): lax.ppermute(lax.slice_in_dim(block, 0, width, axis=dim), axis, backward)  185 us
    all_to_all x4, waiting for transfers between devices, on_device(): lax.all_to_all(local_snap, 'gx', split_axis=2, concat_axis=3, tiled=True)  31.4 us
    ppermute x72, waiting for transfers between devices, extended(): lax.ppermute(lax.slice_in_dim(block, block.shape[dim] - width, None, axis...  26.8 us
  transfers between devices with their start and end apart: 149, of which 96 were waited for; matrix products, arithmetic and copies ran while one was open for 1% of the time, Pallas kernels for 0%

commit v1 on v0

--- a/solution.py
+++ b/solution.py
@@ -100,7 +100,7 @@
     local_gram = lax.dot_general(
         sketch_rows, sketch_rows, (((0,), (0,)), ((), ())), precision=HIGHEST
     )
-    gram_sum = lax.psum(local_gram, ("gx", "gy", "gz"))
+    gram_sum = jnp.sum(lax.all_gather(local_gram, ("gx", "gy", "gz")), axis=0)
     lower_factor = jnp.linalg.cholesky(gram_sum)
     identity = jnp.eye(rank_total, dtype=jnp.float32)
     inverse = lax.linalg.triangular_solve(lower_factor, identity, left_side=True, lower=True).T

time: 1310 us -> 1720 us (1.31)
  waiting for transfers between devices: 687 us -> 1080 us
    all_gather x0 -> x1, waiting for transfers between devices: none -> 840 us  [on_device(): gram_sum = jnp.sum(lax.all_gather(local_gram, ('gx', 'gy', 'gz')), axis=0)]
    psum x1 -> x0, waiting for transfers between devices: 444 us -> none  [on_device(): gram_sum = lax.psum(local_gram, ('gx', 'gy', 'gz'))]
  transfers between devices with their start and end apart: 149 -> 149, of which waited for: 96 -> 97; matrix products, arithmetic and copies ran while one was open for 1% -> 1% of each run, Pallas kernels for 0% -> 0%
where the time goes in v1:
time: 1720 us; the launch traced here: 1700 us
  waiting for transfers between devices  1080 us (63%)
  starting transfers between devices  523 us (30%)
  other arithmetic  54.9 us (3%)
  between operations  18.1 us (1%)
    all_gather x1, waiting for transfers between devices, on_device(): gram_sum = jnp.sum(lax.all_gather(local_gram, ('gx', 'gy', 'gz')), axis=0)  840 us
    ppermute x72, starting transfers between devices, extended(): lax.ppermute(lax.slice_in_dim(block, 0, width, axis=dim), axis, backward)  267 us
    ppermute x72, starting transfers between devices, extended(): lax.ppermute(lax.slice_in_dim(block, block.shape[dim] - width, None, axis...  231 us
    ppermute x72, waiting for transfers between devices, extended(): lax.ppermute(lax.slice_in_dim(block, 0, width, axis=dim), axis, backward)  186 us
  transfers between devices with their start and end apart: 149, of which 97 were waited for; matrix products, arithmetic and copies ran while one was open for 1% of the time, Pallas kernels for 0%

profile of v1, /device:TPU:1, one launch (start us, length us, event | category | flops | bytes accessed | tf_op | source)
XLA Modules:
  0.0 1702.0 jit_solution(11728703029529781759)
XLA Ops:
  12.3 9.5 collective-permute-start.1
  31.3 7.0 collective-permute-start.4
  41.4 5.9 collective-permute-done.5
  50.0 5.1 collective-permute-start.7
  71.5 5.9 collective-permute-done.11
  80.1 5.1 collective-permute-start.13
  88.3 5.2 collective-permute-start.15
  101.7 5.9 collective-permute-done.17
  110.4 5.0 collective-permute-start.19
  119.0 4.6 collective-permute-start.21
  131.8 5.9 collective-permute-done.23
  148.8 5.4 collective-permute-start.27
  162.7 5.9 collective-permute-done.29
  169.4 4.9 collective-permute-start.30
  181.3 5.1 collective-permute-start.33
  194.8 5.9 collective-permute-done.35
  211.8 5.5 collective-permute-start.39
  225.8 5.9 collective-permute-done.41
  242.4 5.5 collective-permute-start.45
  248.9 4.6 collective-permute-start.46
  256.7 5.9 collective-permute-done.47
  272.6 5.5 collective-permute-start.51
  279.1 4.6 collective-permute-start.52
  286.8 5.9 collective-permute-done.53
  303.0 5.5 collective-permute-start.57
  316.9 5.9 collective-permute-done.59
  333.2 5.4 collective-permute-start.63
  347.0 5.9 collective-permute-done.65
  363.3 5.5 collective-permute-start.69
  369.8 4.6 collective-permute-start.70
  377.5 5.9 collective-permute-done.71
  393.4 5.5 collective-permute-start.75
  407.6 5.9 collective-permute-done.77
  423.8 5.5 collective-permute-start.81
  437.8 5.9 collective-permute-done.83
  454.0 5.4 collective-permute-start.87
  467.9 5.9 collective-permute-done.89
  484.1 5.5 collective-permute-start.93
  498.0 5.9 collective-permute-done.95
  514.2 5.5 collective-permute-start.99
  528.1 5.9 collective-permute-done.101
  544.3 5.5 collective-permute-start.105
  558.2 5.9 collective-permute-done.107
  574.4 5.5 collective-permute-start.111
  588.4 5.9 collective-permute-done.113
  604.9 5.7 collective-permute-start.117
  619.0 5.9 collective-permute-done.119
  636.0 5.5 collective-permute-start.123
  649.9 5.9 collective-permute-done.125
  666.9 5.5 collective-permute-start.129
  680.8 5.9 collective-permute-done.131
  697.8 5.5 collective-permute-start.135
  711.7 5.9 collective-permute-done.137
  725.6 6.0 all-to-all-start
  734.6 5.5 collective-permute-start.141
  748.2 5.9 collective-permute-done.143
  754.6 11.8 all-to-all-start.1
  767.6 11.0 all-to-all-done.1
  782.9 11.6 all-to-all-done.2
  801.9 8.5 all-to-all-done.3
  815.6 840.0 %all-gather.3.cloned.1.call-done = f32[65536,128]{1,0:T(8,128)} async-done(((f32[128,128]{1,0:T(8,128)}), f32[65536,128]{1,0:T(8,128)}) %all-gather.3.cloned.1.call-update) | async-done | bytes 33554448 | tf_op jit(solution)/shard_map/all_gather | solution.py:103
  1655.5 13.4 reduce_sum.49
  1669.0 11.7 cholesky.17
  1682.2 9.8 custom-call.6
  (460 shorter events, 449.4 us)
Async XLA Ops:
  8.0 13.9 collective-permute-start
  12.3 10.4 collective-permute-start.1
  22.8 7.5 collective-permute-start.2
  31.3 10.1 collective-permute-start.4
  38.3 9.0 collective-permute-start.5
  56.0 7.4 collective-permute-start.8
  68.4 9.0 collective-permute-start.11
  86.1 7.4 collective-permute-start.14
  98.5 9.0 collective-permute-start.17
  128.7 9.0 collective-permute-start.23
  155.3 7.4 collective-permute-start.28
  159.6 9.0 collective-permute-start.29
  179.0 7.4 collective-permute-start.32
  187.4 7.4 collective-permute-start.34
  191.7 9.0 collective-permute-start.35
  218.3 7.4 collective-permute-start.40
  222.6 9.0 collective-permute-start.41
  248.9 7.7 collective-permute-start.46
  253.5 9.0 collective-permute-start.47
  279.1 7.7 collective-permute-start.52
  283.7 9.0 collective-permute-start.53
  309.5 7.4 collective-permute-start.58
  313.8 9.0 collective-permute-start.59
  331.2 7.4 collective-permute-start.62
  339.6 7.4 collective-permute-start.64
  343.9 9.0 collective-permute-start.65
  369.8 7.7 collective-permute-start.70
  374.4 9.0 collective-permute-start.71
  399.9 7.7 collective-permute-start.76
  404.5 9.0 collective-permute-start.77
  430.3 7.4 collective-permute-start.82
  434.6 9.0 collective-permute-start.83
  452.0 7.4 collective-permute-start.86
  460.5 7.4 collective-permute-start.88
  464.8 9.0 collective-permute-start.89
  482.2 7.4 collective-permute-start.92
  490.6 7.4 collective-permute-start.94
  494.9 9.0 collective-permute-start.95
  520.7 7.4 collective-permute-start.100
  525.0 9.0 collective-permute-start.101
  550.8 7.4 collective-permute-start.106
  555.1 9.0 collective-permute-start.107
  580.9 7.4 collective-permute-start.112
  585.2 9.0 collective-permute-start.113
  603.0 7.6 collective-permute-start.116
  611.6 7.4 collective-permute-start.118
  615.9 9.0 collective-permute-start.119
  634.1 7.4 collective-permute-start.122
  642.5 7.4 collective-permute-start.124
  646.8 9.0 collective-permute-start.125
  665.0 7.4 collective-permute-start.128
  673.4 7.4 collective-permute-start.130
  677.7 9.0 collective-permute-start.131
  704.3 7.4 collective-permute-start.136
  708.6 9.0 collective-permute-start.137
  718.4 14.2 collective-permute-start.138
  722.0 10.6 collective-permute-start.139
  725.6 29.0 %all-to-all-start = ((f32[3,8,32,2]{1,3,0,2:T(2,128)}), f32[3,8,32,2]{1,3,0,2:T(2,128)S(1)}, u32[]{:S(2)}, u32[]{:S(2)}) async-start(f32[3,8,32,2]{1,3,0,2:T(2,128)} %copy.38), calls=%async_computation | async-start | bytes 196608 | tf_op jit(solution)/shard_map/all_to_all | solution.py:89
  732.6 9.1 collective-permute-start.140
  745.1 9.0 collective-permute-start.143
  754.6 24.0 %all-to-all-start.1 = ((f32[3,8,32,2]{1,3,0,2:T(2,128)}), f32[3,8,32,2]{1,3,0,2:T(2,128)S(1)}, u32[]{:S(2)}, u32[]{:S(2)}) async-start(f32[3,8,32,2]{1,3,0,2:T(2,128)} %copy.42), calls=%async_computation.1 | async-start | bytes 196608 | tf_op jit(solution)/shard_map/all_to_all | solution.py:89
  778.7 15.8 all-to-all-start.2
  794.5 16.0 all-to-all-start.3
  798.6 857.0 %all-gather.3.cloned.1.call-start = ((), (), s32[]{:S(2)}) async-start(), calls=%async_computation.4 | async-start | bytes 33619968 | tf_op jit(solution)/shard_map/all_gather | solution.py:103
  (90 other events, 644.2 us)
Sparse Core Ops, SparseCore 0:
  815.0 840.4 all-gather.2
